TPU v7x, 256 devices: a whole 4x4x8 slice. The times are simulated.
256 devices in a mesh: row: 8 (over y, core), col: 32 (over z, x).
Axes of the slice: x: 4, y: 4, z: 8, core: 2. Of those that a mesh axis runs over, the one named last changes fastest.
Arguments:
- blocks: float32 [128, 32, 256, 256], P('row', 'col'), may hold values from -6 to 6
- panel_rows: int32 [2, 64], P(None, 'row'), may hold values from -1 to 767, as said below
- target_slots: int32 [2, 128, 32], P(None, 'row', 'col'), may hold values from -1 to 7, as said below
- diag_inverse: float32 [2, 256, 256], replicated, may hold values from -1 to 1, as said below
- cross_block: float32 [256, 256], replicated, may hold values from -6 to 6
Outputs:
- factored: float32 [128, 32, 256, 256], P('row', 'col')
Inputs may be any that keep to these rules, and one draw needn't show every extreme that they name: `panel_rows`: slot q * 2 + m of row device r stands for the m-th structure row of block column class r + q times the number of row devices; both lists are -1 where that class is 0 or 1, and list 0 is -1 also where block column 0 lacks the row; otherwise list 0 equals list 1. `target_slots`: A filled slot of class c names in entry 0 a slot of its own row device and in entry 1 a slot of row device c modulo the number of row devices, within (c // number of row devices) * 2 and the 1 after it; both are filled or both -1, always -1 in classes 0 and 1; the target's block row number is at least its block column number. `diag_inverse`: each matrix is lower triangular.
All inputs are finite; a program needn't handle non-finite values.
Results may differ from a plain program's by a relative error of at most 0.0003.
Values sent between devices are 32-bit elements; how exact they have to be, the bound alone decides.
No kernel may reach another device: no remote copies, remote signals or barrier semaphores. Data moves between devices by JAX's collectives and lax.ppermute only.
A program may use at most 128 MiB of HBM per device.

v0:
```python
import jax
import jax.numpy as jnp
import numpy as np
from jax import lax
from jax.sharding import Mesh
from jax.sharding import PartitionSpec as P

PER_CLASS = 2
X_SIZE = 4
HIGHEST_PRECISION = lax.Precision.HIGHEST
PRODUCT_PRECISION = lax.Precision.HIGH
COL_AXES = ("zh", "zl", "x")
CLASS_AXES = ("zl", "x")


def apply_inverse(panel_rows_block, inverse):
    return jnp.einsum("ab,cb->ac", panel_rows_block, inverse, precision=HIGHEST_PRECISION)


def per_device(blocks, panel_rows, target_slots, diag_inverse, cross_block):
    row_count = lax.axis_size("row")
    col_count = lax.axis_size(COL_AXES)
    column = lax.axis_index(COL_AXES)
    stored = blocks[:, 0]
    slot_count = panel_rows.shape[1]
    block = stored.shape[-1]
    head_part = stored[:slot_count]
    chunk = slot_count * block // col_count
    pieces = head_part.reshape(col_count, chunk, block)
    received = lax.all_to_all(pieces, COL_AXES, 0, 0, tiled=True)
    zero_rows = received[0]
    one_rows = received[1]
    piece_slot = column * chunk // block
    first_live = lax.dynamic_index_in_dim(panel_rows[0], piece_slot, keepdims=False) >= 0
    second_live = lax.dynamic_index_in_dim(panel_rows[1], piece_slot, keepdims=False) >= 0
    cross_factor = jnp.dot(cross_block, diag_inverse[0].T, precision=HIGHEST_PRECISION)
    first_piece = jnp.where(first_live, apply_inverse(zero_rows, diag_inverse[0]), 0.0)
    updated_piece = one_rows - apply_inverse(first_piece, cross_factor)
    second_piece = jnp.where(second_live, apply_inverse(updated_piece, diag_inverse[1]), 0.0)
    both_pieces = jnp.stack([first_piece, second_piece])
    class_size = lax.axis_size(CLASS_AXES)
    swap = [
        (a * class_size + b, b * class_size + a)
        for a in range(row_count)
        for b in range(class_size)
    ]
    swapped = lax.ppermute(both_pieces, ("row",) + CLASS_AXES, swap)
    spread = jnp.broadcast_to(swapped[None], (row_count,) + swapped.shape)
    class_pieces = lax.all_to_all(spread, "row", 0, 0, tiled=True)
    per_slot = block // chunk
    class_pieces = class_pieces.reshape(PER_CLASS, per_slot, 2, chunk, block)
    both_cols = class_pieces.transpose(2, 0, 1, 3, 4).reshape(2, PER_CLASS, block, block)
    both_rows = lax.all_gather(both_pieces, "x", axis=1, tiled=True)
    both_rows = lax.all_gather(both_rows, ("zh", "zl"), axis=1, tiled=True)
    both_rows = both_rows.reshape(2, slot_count, block, block)
    first_rows = both_rows[0]
    second_rows = both_rows[1]
    class_start = column // row_count * PER_CLASS
    row_index = target_slots[0, :, 0]
    col_index = target_slots[1, :, 0]
    present = row_index >= 0
    left_slot = jnp.where(present, row_index, 0)
    right_slot = jnp.where(present, col_index - class_start, 0)
    products = jnp.einsum("fakm,fbjm->akbj", both_rows, both_cols, precision=PRODUCT_PRECISION)
    schur_term = products[left_slot, :, right_slot, :]
    trailing = stored - jnp.where(present[:, None, None], schur_term, 0.0)
    head_live = panel_rows >= 0
    keep_mask = ((column == 0) & head_live[0] | (column == 1) & head_live[1])[:, None, None]
    own_panel = jnp.where(column == 0, first_rows, second_rows)
    head_blocks = jnp.where(keep_mask, own_panel, trailing[:slot_count])
    factored = jnp.concatenate([head_blocks, trailing[slot_count:]], axis=0)
    return factored[:, None]


def solution(mesh):
    row_count = mesh.shape["row"]
    col_count = mesh.shape["col"]
    devices = np.asarray(mesh.devices).reshape(
        row_count, col_count // row_count, row_count // X_SIZE, X_SIZE
    )
    split_mesh = Mesh(devices, ("row",) + COL_AXES)
    return jax.shard_map(
        per_device,
        mesh=split_mesh,
        in_specs=(
            P("row", COL_AXES, None, None),
            P(None, "row"),
            P(None, "row", COL_AXES),
            P(),
            P(),
        ),
        out_specs=P("row", COL_AXES, None, None),
        check_vma=False,
    )
```

profile of v0, /device:TPU:1, one launch (start us, length us, event | category | flops | bytes accessed | tf_op | source)
XLA Modules:
  0.0 167.1 jit_solution(10187118807811461021)
XLA Ops:
  6.5 0.0 copy-start
  6.5 0.0 copy-start.4
  6.5 0.0 copy-start.2
  6.5 3.1 %slice.52 = f32[8,1,256,256]{3,2,1,0:T(8,128)} slice(f32[16,1,256,256]{3,2,1,0:T(8,128)} %param.5), slice={[0:8], [0:1], [0:256], [0:256]} | slice | bytes 4194304 | tf_op jit(solution)/shard_map/slice | solution.py:27
  9.7 11.9 %all-to-all-start = ((f32[32,64,256]{2,1,0:T(8,128)}), f32[32,64,256]{2,1,0:T(8,128)S(1)}, u32[]{:S(2)}, u32[]{:S(2)}) async-start(f32[32,64,256]{2,1,0:T(8,128)} %bitcast.2), calls=%async_computation | async-start | bytes 4194304 | tf_op jit(solution)/shard_map/all_to_all | solution.py:30
  21.5 0.0 copy-start.3
  21.5 0.0 all-gather.2.cloned.1.call-start
  21.6 0.0 copy-done.4
  21.6 0.7 fusion.18
  22.3 0.0 copy-done
  22.3 0.0 copy-done.2
  22.3 0.4 fusion.7
  22.7 47.3 %all-to-all-done = f32[32,64,256]{2,1,0:T(8,128)S(1)} async-done(((f32[32,64,256]{2,1,0:T(8,128)}), f32[32,64,256]{2,1,0:T(8,128)S(1)}, u32[]{:S(2)}, u32[]{:S(2)}) %all-to-all-start) | async-done | bytes 2097184 | tf_op jit(solution)/shard_map/all_to_all | solution.py:30
  70.0 1.0 convolution_select_fusion.1
  71.0 0.4 convolution_subtract_fusion
  71.4 1.0 fusion.5
  72.4 13.8 %all_gather.6 = f32[2,256,256]{2,1,0:T(8,128)} all-gather(f32[2,64,256]{2,1,0:T(8,128)S(1)} %pad_maximum_fusion), channel_id=1, replica_groups=mesh['row'=8,'zh'=4,'zl'=2,'x'=4] {'x'}, dimensions={1}, use_global_device_ids=true | all-gather | bytes 655360 | tf_op jit(solution)/shard_map/all_gather | solution.py:53
  86.2 0.0 all-gather.2.cloned.1.call-update
  86.2 6.0 %collective-permute-start = (f32[2,64,256]{2,1,0:T(8,128)S(1)}, f32[2,64,256]{2,1,0:T(8,128)S(1)}, u32[]{:S(2)}, u32[]{:S(2)}) collective-permute-start(f32[2,64,256]{2,1,0:T(8,128)S(1)} %pad_maximum_fusion), channel_id=1, source_target_pairs={{0,0},{1,32},{2,64},{3,96},{4,128},{5,160},{6,192},{7,224},{32,1},... | collective-permute-start | bytes 393224 | tf_op jit(solution)/shard_map/ppermute | solution.py:47
  92.2 2.6 %collective-permute-done = f32[2,64,256]{2,1,0:T(8,128)S(1)} collective-permute-done((f32[2,64,256]{2,1,0:T(8,128)S(1)}, f32[2,64,256]{2,1,0:T(8,128)S(1)}, u32[]{:S(2)}, u32[]{:S(2)}) %collective-permute-start) | collective-permute-done | bytes 131104 | tf_op jit(solution)/shard_map/ppermute | solution.py:47
  94.8 1.1 broadcast_in_dim.44
  95.9 10.8 %all-to-all-start.1 = ((f32[8,2,64,256]{3,2,1,0:T(8,128)}), f32[8,2,64,256]{3,2,1,0:T(8,128)S(1)}, u32[]{:S(2)}, u32[]{:S(2)}) async-start(f32[8,2,64,256]{3,2,1,0:T(8,128)} %broadcast_in_dim.44), calls=%async_computation.1 | async-start | bytes 2097152 | tf_op jit(solution)/shard_map/all_to_all | solution.py:49
  106.7 0.0 copy-done.3
  106.8 15.0 %all-to-all-done.1 = f32[8,2,64,256]{3,2,1,0:T(8,128)S(1)} async-done(((f32[8,2,64,256]{3,2,1,0:T(8,128)}), f32[8,2,64,256]{3,2,1,0:T(8,128)S(1)}, u32[]{:S(2)}, u32[]{:S(2)}) %all-to-all-start.1) | async-done | bytes 1048608 | tf_op jit(solution)/shard_map/all_to_all | solution.py:49
  121.8 0.1 copy.8
  121.9 18.3 %all-gather.2.cloned.1.call-done = f32[2,2048,256]{2,1,0:T(8,128)} async-done(((f32[2,256,256]{2,1,0:T(8,128)}), f32[2,2048,256]{2,1,0:T(8,128)}) %all-gather.2.cloned.1.call-update) | async-done | bytes 4194320 | tf_op jit(solution)/shard_map/all_gather | solution.py:54
  140.3 7.2 %fusion.2 = f32[8,256,2,256]{3,1,2,0:T(8,128)} fusion(f32[2,2,256,256,1]{3,2,0,1,4:T(8,128)S(1)} %bitcast.66, f32[2,8,256,256,1]{3,2,1,0,4:T(8,128)} %bitcast.64), kind=kOutput, calls=%fused_computation.5 | convolution fusion | flops 3221225472 | bytes 9437184 | tf_op jit(solution)/shard_map/fakm,fbjm->akbj/dot_general | solution.py:64
  147.5 5.0 %gather_fusion = f32[16,256,256]{2,1,0:T(8,128)} fusion(f32[8,256,2,256]{3,1,2,0:T(8,128)} %fusion.2, s32[16]{0:T(128)S(1)} %fusion.16), kind=kCustom, calls=%fused_computation | custom fusion | bytes 8388736 | tf_op jit(solution)/shard_map/gather | solution.py:65
  152.4 0.0 copy-start.1
  152.4 4.2 %bitcast_subtract_fusion = f32[16,256,256]{2,1,0:T(8,128)S(1)} fusion(f32[16,1,256,256]{3,2,1,0:T(8,128)} %param.5, f32[16,256,256]{2,1,0:T(8,128)} %gather_fusion, pred[16]{0:T(512)(128)(4,1)S(1)} %compare_bitcast_fusion), kind=kLoop, calls=%fused_computation.4 | loop fusion | flops 2097152 | bytes 12582928 | tf_op jit(solution)/shard_map/sub | solution.py:66
  156.7 0.4 copy-done.1
  157.1 0.3 slice_select_fusion.1
  157.4 0.4 slice_select_fusion
  157.8 2.4 %maximum_bitcast_fusion = f32[16,1,256,256]{3,2,1,0:T(8,128)} fusion(f32[8,256,256]{2,1,0:T(8,128)S(1)} %get-tuple-element.6, f32[8,256,256]{2,1,0:T(8,128)S(1)} %get-tuple-element.5), kind=kLoop, calls=%fused_computation.1 | loop fusion | flops 1048576 | bytes 8388608 | tf_op jit(solution)/shard_map/broadcast_in_dim | solution.py:72
  (6 shorter events, 0.1 us)
Async XLA Ops:
  6.5 15.8 %copy-start = (f32[256,256]{1,0:T(8,128)S(1)}, f32[256,256]{1,0:T(8,128)}, u32[]{:S(2)}) copy-start(f32[256,256]{1,0:T(8,128)} %param.9) | copy-start | bytes 786436
  6.5 15.1 %copy-start.4 = (s32[2,8]{1,0:T(2,128)S(1)}, s32[2,8]{1,0:T(2,128)}, u32[]{:S(2)}) copy-start(s32[2,8]{1,0:T(2,128)} %param.6) | copy-start | bytes 196
  6.5 15.8 %copy-start.2 = (f32[2,256,256]{2,1,0:T(8,128)S(1)}, f32[2,256,256]{2,1,0:T(8,128)}, u32[]{:S(2)}) copy-start(f32[2,256,256]{2,1,0:T(8,128)} %param.8) | copy-start | bytes 1572868
  9.7 60.4 %all-to-all-start = ((f32[32,64,256]{2,1,0:T(8,128)}), f32[32,64,256]{2,1,0:T(8,128)S(1)}, u32[]{:S(2)}, u32[]{:S(2)}) async-start(f32[32,64,256]{2,1,0:T(8,128)} %bitcast.2), calls=%async_computation | async-start | bytes 4194304 | tf_op jit(solution)/shard_map/all_to_all | solution.py:30
  21.5 85.2 %copy-start.3 = (s32[2,16,1]{1,2,0:T(1,128)S(1)}, s32[2,16,1]{1,2,0:T(1,128)}, u32[]{:S(2)}) copy-start(s32[2,16,1]{1,2,0:T(1,128)} %param.7) | copy-start | bytes 388
  21.5 118.7 %all-gather.2.cloned.1.call-start = ((), (), s32[]{:S(2)}) async-start(), calls=%async_computation.2 | async-start | bytes 4718592 | tf_op jit(solution)/shard_map/all_gather | solution.py:54
  86.2 8.6 %collective-permute-start = (f32[2,64,256]{2,1,0:T(8,128)S(1)}, f32[2,64,256]{2,1,0:T(8,128)S(1)}, u32[]{:S(2)}, u32[]{:S(2)}) collective-permute-start(f32[2,64,256]{2,1,0:T(8,128)S(1)} %pad_maximum_fusion), channel_id=1, source_target_pairs={{0,0},{1,32},{2,64},{3,96},{4,128},{5,160},{6,192},{7,224},{32,1},... | collective-permute-start | bytes 393224 | tf_op jit(solution)/shard_map/ppermute | solution.py:47
  95.9 25.9 %all-to-all-start.1 = ((f32[8,2,64,256]{3,2,1,0:T(8,128)}), f32[8,2,64,256]{3,2,1,0:T(8,128)S(1)}, u32[]{:S(2)}, u32[]{:S(2)}) async-start(f32[8,2,64,256]{3,2,1,0:T(8,128)} %broadcast_in_dim.44), calls=%async_computation.1 | async-start | bytes 2097152 | tf_op jit(solution)/shard_map/all_to_all | solution.py:49
  152.4 4.6 %copy-start.1 = (f32[2,2048,256]{2,1,0:T(8,128)S(1)}, f32[2,2048,256]{2,1,0:T(8,128)}, u32[]{:S(2)}) copy-start(f32[2,2048,256]{2,1,0:T(8,128)} %all-gather.2.cloned.1.call-done) | copy-start | bytes 12582916
Sparse Core Ops, SparseCore 0:
  86.3 53.9 all-gather.1
where the time goes:
time: 167 us
  waiting for transfers between devices  83.3 us (50%)
  starting transfers between devices  28.7 us (17%)
  blocking collectives  13.8 us (8%)
  between operations  13.5 us (8%)
  matrix products  9.97 us (6%)
  local copies, waits for them, and re-layouts  9.68 us (6%)
  other arithmetic  8.07 us (5%)
    all_to_all x1, waiting for transfers between devices, per_device(): received = lax.all_to_all(pieces, COL_AXES, 0, 0, tiled=True)  47.3 us
    all_gather x1, waiting for transfers between devices, per_device(): both_rows = lax.all_gather(both_rows, ('zh', 'zl'), axis=1, tiled=True)  18.3 us
    all_to_all x1, waiting for transfers between devices, per_device(): class_pieces = lax.all_to_all(spread, 'row', 0, 0, tiled=True)  15 us
    all_gather x1, blocking collectives, per_device(): both_rows = lax.all_gather(both_pieces, 'x', axis=1, tiled=True)  13.8 us
    all_to_all x1, starting transfers between devices, per_device(): received = lax.all_to_all(pieces, COL_AXES, 0, 0, tiled=True)  11.9 us
    all_to_all x1, starting transfers between devices, per_device(): class_pieces = lax.all_to_all(spread, 'row', 0, 0, tiled=True)  10.8 us
    dot_general x1, matrix products, per_device(): jnp.einsum('fakm,fbjm->akbj', both_rows, both_cols, precision=PRODUCT_PRE...  7.19 us
    ppermute x1, starting transfers between devices, per_device(): swapped = lax.ppermute(both_pieces, ('row',) + CLASS_AXES, swap)  5.96 us
  transfers between devices with their start and end apart: 4, of which 4 were waited for; matrix products, arithmetic and copies ran while one was open for 1% of the time, Pallas kernels for 0%

commit v1 on v0

--- a/solution.py
+++ b/solution.py
@@ -51,7 +51,10 @@
     class_pieces = class_pieces.reshape(PER_CLASS, per_slot, 2, chunk, block)
     both_cols = class_pieces.transpose(2, 0, 1, 3, 4).reshape(2, PER_CLASS, block, block)
     both_rows = lax.all_gather(both_pieces, "x", axis=1, tiled=True)
-    both_rows = lax.all_gather(both_rows, ("zh", "zl"), axis=1, tiled=True)
+    both_rows = jnp.concatenate(
+        lax.all_to_all(jnp.stack([both_rows] * lax.axis_size(("zh", "zl"))), ("zh", "zl"), 0, 0),
+        axis=1,
+    )
     both_rows = both_rows.reshape(2, slot_count, block, block)
     first_rows = both_rows[0]
     second_rows = both_rows[1]

time: 167 us -> 224 us (1.34); the launches traced: 167 us -> 221 us
  waiting for transfers between devices: 83.3 us -> 145 us
  between operations: 13.5 us -> 0.17 us
  starting transfers between devices: 28.7 us -> 32.5 us
  blocking collectives: 13.8 us -> 11.2 us
    all_to_all x0 -> x1, waiting for transfers between devices: none -> 91.2 us  [per_device(): lax.all_to_all(jnp.stack([both_rows] * lax.axis_size(('zh', 'zl'))), ('zh...]
    all_gather x1 -> x0, waiting for transfers between devices: 18.3 us -> none  [per_device(): both_rows = lax.all_gather(both_rows, ('zh', 'zl'), axis=1, tiled=True)]
    all_to_all x1, waiting for transfers between devices: 15 us -> 3.87 us  [per_device(): class_pieces = lax.all_to_all(spread, 'row', 0, 0, tiled=True)]
    all_to_all x0 -> x1, starting transfers between devices: none -> 4.68 us  [per_device(): lax.all_to_all(jnp.stack([both_rows] * lax.axis_size(('zh', 'zl'))), ('zh...]
    select_n x1, other arithmetic: 0.43 us -> 2.97 us  [per_device(): head_blocks = jnp.where(keep_mask, own_panel, trailing[:slot_count])]
    all_gather x1, blocking collectives: 13.8 us -> 11.2 us  [per_device(): both_rows = lax.all_gather(both_pieces, 'x', axis=1, tiled=True)]
    another operation x0 -> x1, local copies, waits for them, and re-layouts: none -> 2.42 us  [per_device(): jnp.stack([both_rows] * lax.axis_size(('zh', 'zl')))]
where the time goes in v1:
time: 224 us; the launch traced here: 221 us
  waiting for transfers between devices  145 us (65%)
  starting transfers between devices  32.5 us (15%)
  local copies, waits for them, and re-layouts  11.7 us (5%)
  blocking collectives  11.2 us (5%)
  other arithmetic  10.2 us (5%)
  matrix products  9.9 us (4%)
    all_to_all x1, waiting for transfers between devices, per_device(): lax.all_to_all(jnp.stack([both_rows] * lax.axis_size(('zh', 'zl'))), ('zh...  91.2 us
    all_to_all x1, waiting for transfers between devices, per_device(): received = lax.all_to_all(pieces, COL_AXES, 0, 0, tiled=True)  47.4 us
    all_to_all x1, starting transfers between devices, per_device(): received = lax.all_to_all(pieces, COL_AXES, 0, 0, tiled=True)  11.9 us
    all_gather x1, blocking collectives, per_device(): both_rows = lax.all_gather(both_pieces, 'x', axis=1, tiled=True)  11.2 us
    all_to_all x1, starting transfers between devices, per_device(): class_pieces = lax.all_to_all(spread, 'row', 0, 0, tiled=True)  10.9 us
    dot_general x1, matrix products, per_device(): jnp.einsum('fakm,fbjm->akbj', both_rows, both_cols, precision=PRODUCT_PRE...  7.19 us
    ppermute x1, starting transfers between devices, per_device(): swapped = lax.ppermute(both_pieces, ('row',) + CLASS_AXES, swap)  5.02 us
    gather x1, local copies, waits for them, and re-layouts, per_device(): schur_term = products[left_slot, :, right_slot, :]  4.98 us
  transfers between devices with their start and end apart: 4, of which 4 were waited for; matrix products, arithmetic and copies ran while one was open for 1% of the time, Pallas kernels for 0%

profile of v1, /device:TPU:1, one launch (start us, length us, event | category | flops | bytes accessed | tf_op | source)
XLA Modules:
  0.0 220.7 jit_solution(2542515000111328102)
XLA Ops:
  0.0 0.0 copy-start
  0.0 0.0 copy-start.3
  0.0 0.0 copy-start.1
  0.0 3.1 %slice.50 = f32[8,1,256,256]{3,2,1,0:T(8,128)} slice(f32[16,1,256,256]{3,2,1,0:T(8,128)} %param.5), slice={[0:8], [0:1], [0:256], [0:256]} | slice | bytes 4194304 | tf_op jit(solution)/shard_map/slice | solution.py:27
  3.1 11.9 %all-to-all-start = ((f32[32,64,256]{2,1,0:T(8,128)}), f32[32,64,256]{2,1,0:T(8,128)S(1)}, u32[]{:S(2)}, u32[]{:S(2)}) async-start(f32[32,64,256]{2,1,0:T(8,128)} %bitcast.2), calls=%async_computation | async-start | bytes 4194304 | tf_op jit(solution)/shard_map/all_to_all | solution.py:30
  15.0 0.0 copy-done.3
  15.1 0.6 fusion.19
  15.7 0.0 copy-done
  15.7 0.0 copy-done.1
  15.7 0.4 fusion.8
  16.1 47.4 %all-to-all-done = f32[32,64,256]{2,1,0:T(8,128)S(1)} async-done(((f32[32,64,256]{2,1,0:T(8,128)}), f32[32,64,256]{2,1,0:T(8,128)S(1)}, u32[]{:S(2)}, u32[]{:S(2)}) %all-to-all-start) | async-done | bytes 2097184 | tf_op jit(solution)/shard_map/all_to_all | solution.py:30
  63.5 0.9 convolution_select_fusion.1
  64.4 0.4 convolution_subtract_fusion
  64.8 1.0 fusion.6
  65.8 5.0 %collective-permute-start = (f32[2,64,256]{2,1,0:T(8,128)S(1)}, f32[2,64,256]{2,1,0:T(8,128)S(1)}, u32[]{:S(2)}, u32[]{:S(2)}) collective-permute-start(f32[2,64,256]{2,1,0:T(8,128)S(1)} %pad_maximum_fusion), channel_id=1, source_target_pairs={{0,0},{1,32},{2,64},{3,96},{4,128},{5,160},{6,192},{7,224},{32,1},... | collective-permute-start | bytes 393224 | tf_op jit(solution)/shard_map/ppermute | solution.py:47
  70.8 2.6 %collective-permute-done = f32[2,64,256]{2,1,0:T(8,128)S(1)} collective-permute-done((f32[2,64,256]{2,1,0:T(8,128)S(1)}, f32[2,64,256]{2,1,0:T(8,128)S(1)}, u32[]{:S(2)}, u32[]{:S(2)}) %collective-permute-start) | collective-permute-done | bytes 131104 | tf_op jit(solution)/shard_map/ppermute | solution.py:47
  73.5 1.1 broadcast_in_dim.44
  74.5 10.9 %all-to-all-start.2 = ((f32[8,2,64,256]{3,2,1,0:T(8,128)}), f32[8,2,64,256]{3,2,1,0:T(8,128)S(1)}, u32[]{:S(2)}, u32[]{:S(2)}) async-start(f32[8,2,64,256]{3,2,1,0:T(8,128)} %broadcast_in_dim.44), calls=%async_computation.2 | async-start | bytes 2097152 | tf_op jit(solution)/shard_map/all_to_all | solution.py:49
  85.5 11.2 %all_gather.3 = f32[2,256,256]{2,1,0:T(8,128)S(1)} all-gather(f32[2,64,256]{2,1,0:T(8,128)S(1)} %pad_maximum_fusion), channel_id=1, replica_groups=mesh['row'=8,'zh'=4,'zl'=2,'x'=4] {'x'}, dimensions={1}, use_global_device_ids=true | all-gather | bytes 655360 | tf_op jit(solution)/shard_map/all_gather | solution.py:53
  96.7 3.9 %all-to-all-done.2 = f32[8,2,64,256]{3,2,1,0:T(8,128)S(1)} async-done(((f32[8,2,64,256]{3,2,1,0:T(8,128)}), f32[8,2,64,256]{3,2,1,0:T(8,128)S(1)}, u32[]{:S(2)}, u32[]{:S(2)}) %all-to-all-start.2) | async-done | bytes 1048608 | tf_op jit(solution)/shard_map/all_to_all | solution.py:49
  100.6 2.4 %stack.11 = f32[8,2,256,256]{3,2,1,0:T(8,128)} broadcast(f32[2,256,256]{2,1,0:T(8,128)S(1)} %all_gather.3), dimensions={1,2,3} | broadcast | bytes 4718592 | tf_op jit(solution)/shard_map/stack | solution.py:55
  103.0 0.0 copy-start.2
  103.0 4.7 %all-to-all-start.1 = ((f32[8,2,256,256]{3,2,1,0:T(8,128)}), f32[8,2,256,256]{3,2,1,0:T(8,128)}, u32[]{:S(2)}, u32[]{:S(2)}) async-start(f32[8,2,256,256]{3,2,1,0:T(8,128)} %stack.11), calls=%async_computation.1 | async-start | bytes 8388608 | tf_op jit(solution)/shard_map/all_to_all | solution.py:55
  107.7 0.0 copy-done.2
  107.8 0.1 copy.7
  107.9 91.2 %all-to-all-done.1 = f32[8,2,256,256]{3,2,1,0:T(8,128)} async-done(((f32[8,2,256,256]{3,2,1,0:T(8,128)}), f32[8,2,256,256]{3,2,1,0:T(8,128)}, u32[]{:S(2)}, u32[]{:S(2)}) %all-to-all-start.1) | async-done | bytes 4194336 | tf_op jit(solution)/shard_map/all_to_all | solution.py:55
  199.0 7.2 %fusion.2 = f32[8,256,2,256]{3,1,2,0:T(8,128)} fusion(f32[2,2,256,256,1]{3,2,0,1,4:T(8,128)S(1)} %bitcast.73, f32[8,2,256,256]{3,2,1,0:T(8,128)} %all-to-all-done.1), kind=kOutput, calls=%fused_computation.5 | convolution fusion | flops 3221225472 | bytes 9437184 | tf_op jit(solution)/shard_map/fakm,fbjm->akbj/dot_general | solution.py:67
  206.2 5.0 %gather_fusion = f32[16,256,256]{2,1,0:T(8,128)} fusion(f32[8,256,2,256]{3,1,2,0:T(8,128)} %fusion.2, s32[16]{0:T(128)S(1)} %fusion.17), kind=kCustom, calls=%fused_computation | custom fusion | bytes 8388736 | tf_op jit(solution)/shard_map/gather | solution.py:68
  211.2 4.1 %bitcast_subtract_fusion = f32[16,256,256]{2,1,0:T(8,128)S(1)} fusion(f32[16,1,256,256]{3,2,1,0:T(8,128)} %param.5, f32[16,256,256]{2,1,0:T(8,128)} %gather_fusion, pred[16]{0:T(512)(128)(4,1)S(1)} %compare_bitcast_fusion), kind=kLoop, calls=%fused_computation.4 | loop fusion | flops 2097152 | bytes 12582928 | tf_op jit(solution)/shard_map/sub | solution.py:69
  215.3 3.0 %slice_select_fusion = (f32[8,256,256]{2,1,0:T(8,128)S(1)}, f32[8,256,256]{2,1,0:T(8,128)S(1)}) fusion(f32[16,256,256]{2,1,0:T(8,128)S(1)} %bitcast_subtract_fusion, f32[2,8,256,256]{3,2,0,1:T(8,128)} %bitcast.10, pred[8]{0:T(512)(128)(4,1)S(1)} %or_bitcast_fusion, pred[]{:T(512)S(6)} %eq.7), kind=kLoop, calls=%fused_computation.6 | loop fusion | flops 1048576 | bytes 12582921 | tf_op jit(solution)/shard_map/jit(_where)/select_n | solution.py:73
  218.3 2.4 %maximum_bitcast_fusion = f32[16,1,256,256]{3,2,1,0:T(8,128)} fusion(f32[8,256,256]{2,1,0:T(8,128)S(1)} %get-tuple-element.6, f32[8,256,256]{2,1,0:T(8,128)S(1)} %get-tuple-element.5), kind=kLoop, calls=%fused_computation.1 | loop fusion | flops 1048576 | bytes 8388608 | tf_op jit(solution)/shard_map/broadcast_in_dim | solution.py:75
  (6 shorter events, 0.1 us)
Async XLA Ops:
  0.0 15.7 %copy-start = (f32[256,256]{1,0:T(8,128)S(1)}, f32[256,256]{1,0:T(8,128)}, u32[]{:S(2)}) copy-start(f32[256,256]{1,0:T(8,128)} %param.9) | copy-start | bytes 786436
  0.0 15.0 %copy-start.3 = (s32[2,8]{1,0:T(2,128)S(1)}, s32[2,8]{1,0:T(2,128)}, u32[]{:S(2)}) copy-start(s32[2,8]{1,0:T(2,128)} %param.6) | copy-start | bytes 196
  0.0 15.7 %copy-start.1 = (f32[2,256,256]{2,1,0:T(8,128)S(1)}, f32[2,256,256]{2,1,0:T(8,128)}, u32[]{:S(2)}) copy-start(f32[2,256,256]{2,1,0:T(8,128)} %param.8) | copy-start | bytes 1572868
  3.1 60.4 %all-to-all-start = ((f32[32,64,256]{2,1,0:T(8,128)}), f32[32,64,256]{2,1,0:T(8,128)S(1)}, u32[]{:S(2)}, u32[]{:S(2)}) async-start(f32[32,64,256]{2,1,0:T(8,128)} %bitcast.2), calls=%async_computation | async-start | bytes 4194304 | tf_op jit(solution)/shard_map/all_to_all | solution.py:30
  65.8 7.7 %collective-permute-start = (f32[2,64,256]{2,1,0:T(8,128)S(1)}, f32[2,64,256]{2,1,0:T(8,128)S(1)}, u32[]{:S(2)}, u32[]{:S(2)}) collective-permute-start(f32[2,64,256]{2,1,0:T(8,128)S(1)} %pad_maximum_fusion), channel_id=1, source_target_pairs={{0,0},{1,32},{2,64},{3,96},{4,128},{5,160},{6,192},{7,224},{32,1},... | collective-permute-start | bytes 393224 | tf_op jit(solution)/shard_map/ppermute | solution.py:47
  74.5 26.0 %all-to-all-start.2 = ((f32[8,2,64,256]{3,2,1,0:T(8,128)}), f32[8,2,64,256]{3,2,1,0:T(8,128)S(1)}, u32[]{:S(2)}, u32[]{:S(2)}) async-start(f32[8,2,64,256]{3,2,1,0:T(8,128)} %broadcast_in_dim.44), calls=%async_computation.2 | async-start | bytes 2097152 | tf_op jit(solution)/shard_map/all_to_all | solution.py:49
  103.0 4.7 %copy-start.2 = (s32[2,16,1]{1,2,0:T(1,128)S(1)}, s32[2,16,1]{1,2,0:T(1,128)}, u32[]{:S(2)}) copy-start(s32[2,16,1]{1,2,0:T(1,128)} %param.7) | copy-start | bytes 388
  103.0 96.0 %all-to-all-start.1 = ((f32[8,2,256,256]{3,2,1,0:T(8,128)}), f32[8,2,256,256]{3,2,1,0:T(8,128)}, u32[]{:S(2)}, u32[]{:S(2)}) async-start(f32[8,2,256,256]{3,2,1,0:T(8,128)} %stack.11), calls=%async_computation.1 | async-start | bytes 8388608 | tf_op jit(solution)/shard_map/all_to_all | solution.py:55
